TPU v7x, 32 devices: a whole 2x2x4 slice. The times are simulated.
32 devices in a mesh: band: 8 (over y, x, core), date: 4 (over z).
Axes of the slice: x: 2, y: 2, z: 4, core: 2. Of those that a mesh axis runs over, the one named last changes fastest.
Arguments:
- inputs: bfloat16 [8, 32, 128, 512], P('date', 'band'), may hold values from -6 to 6
- preact_one: bfloat16 [8, 32, 128, 512], P('date', 'band'), may hold values from -8 to 8
- preact_two: bfloat16 [8, 32, 128, 512], P('date', 'band'), may hold values from -8 to 8
- cotangent: bfloat16 [8, 32, 128, 512], P('date', 'band'), may hold values from -6 to 6
- weight_one: bfloat16 [3, 3, 512, 512], replicated, may hold values from -0.09375 to 0.09375
- weight_two: bfloat16 [3, 3, 512, 512], replicated, may hold values from -0.09375 to 0.09375
Outputs:
- input_grad: bfloat16 [8, 32, 128, 512], P('date', 'band')
- weight_grad_one: float32 [4608, 512], P('date')
- weight_grad_two: float32 [4608, 512], P('date')
All inputs are finite; a program needn't handle non-finite values.
Results may differ from a plain program's by a relative error of at most 0.0057.
Values may be sent and summed in bfloat16 or wider, within the bound.
No kernel may reach another device: no remote copies, remote signals or barrier semaphores. Data moves between devices by JAX's collectives and lax.ppermute only.
A program may use at most 128 MiB of HBM per device.

v0:
```python
import jax
import jax.numpy as jnp
from jax import lax
from jax.sharding import PartitionSpec as P


def extended(array, sides, width):
    for axis, dim in sides:
        peers, length = (lax.axis_size(axis), array.shape[dim])
        up = [(i, (i + 1) % peers) for i in range(peers - 1)]
        down = [(j, i) for i, j in up]
        last = lax.slice_in_dim(array, length - width, length, axis=dim)
        leading = lax.slice_in_dim(array, 0, width, axis=dim)
        before = lax.ppermute(last, axis, up)
        after = lax.ppermute(leading, axis, down)
        array = jnp.concatenate([before, array, after], axis=dim)
    return array


def slope(field_value):
    logistic = jax.nn.sigmoid(field_value)
    return logistic * (1.0 + field_value * (1.0 - logistic))


def pad_columns(field_value):
    return jnp.pad(field_value, ((0, 0), (0, 0), (1, 1), (0, 0)))


def shifted(padded, row_offset, col_offset, row_count, rim_start):
    col_count = padded.shape[2] - 2
    return padded[
        :,
        rim_start - row_offset : rim_start - row_offset + row_count,
        1 - col_offset : 1 - col_offset + col_count,
        :,
    ]


def weight_terms(left_field, padded, rim_start, grad_scale):
    row_count = left_field.shape[1]
    tap_list = []
    for row_offset in (-1, 0, 1):
        for col_offset in (-1, 0, 1):
            shifted_piece = shifted(padded, row_offset, col_offset, row_count, rim_start)
            tap_list.append(
                lax.dot_general(
                    left_field,
                    shifted_piece,
                    (((0, 1, 2), (0, 1, 2)), ((), ())),
                    preferred_element_type=jnp.float32,
                )
            )
    stacked = jnp.stack(tap_list)
    return (stacked * grad_scale).reshape(-1, stacked.shape[2])


def back_terms(padded, weight, row_count, rim_start):
    accumulated = None
    for row_offset in (-1, 0, 1):
        for col_offset in (-1, 0, 1):
            shifted_piece = shifted(padded, row_offset, col_offset, row_count, rim_start)
            product = lax.dot_general(
                shifted_piece,
                weight[row_offset + 1, col_offset + 1],
                (((3,), (1,)), ((), ())),
                preferred_element_type=jnp.float32,
            )
            accumulated = product if accumulated is None else accumulated + product
    return accumulated


def settle(grad_term):
    share_rows = lax.psum_scatter(grad_term, "date", scatter_dimension=0, tiled=True)
    return lax.psum(share_rows, "band")


def body(inputs, preact_one, preact_two, cotangent, weight_one, weight_two):
    row_count = inputs.shape[1]
    grad_scale = 1.0 / (inputs.shape[0] * lax.axis_size("date"))
    act_one = jax.nn.silu(preact_one.astype(jnp.float32)).astype(jnp.bfloat16)
    delta_two = (cotangent.astype(jnp.float32) * slope(preact_two.astype(jnp.float32))).astype(
        jnp.bfloat16
    )
    padded_two = pad_columns(extended(delta_two, (("band", 1),), 1))
    term_two = weight_terms(act_one, padded_two, 1, grad_scale)
    grad_two = settle(term_two)
    back_one = back_terms(padded_two, weight_two, row_count, 1)
    delta_one = (back_one * slope(preact_one.astype(jnp.float32))).astype(jnp.bfloat16)
    padded_one = pad_columns(extended(delta_one, (("band", 1),), 1))
    term_one = weight_terms(inputs, padded_one, 1, grad_scale)
    grad_one = settle(term_one)
    input_grad = back_terms(padded_one, weight_one, row_count, 1).astype(jnp.bfloat16)
    return (input_grad, grad_one, grad_two)


def solution(mesh):
    placed = (
        P("date", "band", None, None),
        P("date", "band", None, None),
        P("date", "band", None, None),
        P("date", "band", None, None),
        P(),
        P(),
    )
    return jax.shard_map(
        body,
        mesh=mesh,
        in_specs=placed,
        out_specs=(P("date", "band", None, None), P("date", None), P("date", None)),
        check_vma=False,
    )
```

profile of v0, /device:TPU:0, one launch (start us, length us, event | category | flops | bytes accessed | tf_op | source)
XLA Modules:
  0.0 464.7 jit_solution(12425122409398483117)
XLA Ops:
  7.2 2.5 fusion.7
  9.8 1.4 collective-permute-start.1
  11.2 3.0 collective-permute-start
  23.6 4.8 %broadcast_multiply_fusion = f32[9,512,512]{2,1,0:T(8,128)} fusion(f32[9,512,512]{2,1,0:T(8,128)S(1)} %fusion.23), kind=kLoop, calls=%fused_computation.2 | loop fusion | flops 2359296 | bytes 18874368 | tf_op jit(solution)/shard_map/mul | solution.py:54
  28.7 2.2 fusion.109
  31.0 1.8 fusion.43
  32.8 1.8 fusion.39
  38.9 1.7 fusion.14
  42.0 7.8 %collective-permute-start.2 = (bf16[2,1,128,512]{3,2,1,0:T(8,128)(2,1)S(1)}, bf16[2,1,128,512]{3,2,1,0:T(8,128)(2,1)S(1)}, u32[]{:S(2)}, u32[]{:S(2)}) collective-permute-start(bf16[2,1,128,512]{3,2,1,0:T(8,128)(2,1)S(1)} %get-tuple-element.6), channel_id=1, source_target_pairs={{0,4},{4,8},{8,12},{12,16},{16,20},{20,24},{24,28},{1,5},{5,9},{9,... | collective-permute-start | bytes 786440 | tf_op jit(solution)/shard_map/ppermute | solution.py:14
  58.0 4.8 %broadcast_multiply_fusion.1 = f32[9,512,512]{2,1,0:T(8,128)} fusion(f32[9,512,512]{2,1,0:T(8,128)S(1)} %fusion.32), kind=kLoop, calls=%fused_computation.3 | loop fusion | flops 2359296 | bytes 18874368 | tf_op jit(solution)/shard_map/mul | solution.py:54
  63.1 3.6 fusion.99
  66.7 3.1 fusion.93
  69.8 3.1 fusion.59
  72.9 124.7 %reduce-scatter.5.cloned.1.call-done = f32[1152,512]{1,0:T(8,128)} async-done(((f32[4608,512]{1,0:T(8,128)}), f32[1152,512]{1,0:T(8,128)}) %reduce-scatter.5.cloned.1.call-update) | async-done | bytes 2359312 | tf_op jit(solution)/shard_map/reduce_scatter | solution.py:73
  197.6 164.5 %reduce-scatter.3.cloned.1.call-done = f32[1152,512]{1,0:T(8,128)} async-done(((f32[4608,512]{1,0:T(8,128)}), f32[1152,512]{1,0:T(8,128)}) %reduce-scatter.3.cloned.1.call-update) | async-done | bytes 2359312 | tf_op jit(solution)/shard_map/reduce_scatter | solution.py:73
  362.1 2.0 fusion.94
  364.1 1.8 fusion.62
  365.9 1.8 fusion.65
  367.7 1.9 fusion.68
  369.7 1.9 fusion.71
  372.4 3.2 add_convert_fusion
  375.6 77.7 %all-reduce.5.cloned.1.call-done = (f32[1152,512]{1,0:T(8,128)}, f32[1152,512]{1,0:T(8,128)}) async-done(((f32[1152,512]{1,0:T(8,128)}, f32[1152,512]{1,0:T(8,128)}), (f32[1152,512]{1,0:T(8,128)}, f32[1152,512]{1,0:T(8,128)})) %all-reduce.5.cloned.1.call-update) | async-done | bytes 4718608 | tf_op jit(solution)/shard_map/psum | solution.py:74
  453.3 3.4 copy.99
  456.8 1.4 copy.100
  (65 shorter events, 24.4 us)
Async XLA Ops:
  7.2 43.9 %copy-start = (bf16[2,4,128,512]{3,2,1,0:T(8,128)(2,1)S(1)}, bf16[2,4,128,512]{3,2,1,0:T(8,128)(2,1)}, u32[]{:S(2)}) copy-start(bf16[2,4,128,512]{3,2,1,0:T(8,128)(2,1)} %param.6) | copy-start | bytes 3145732
  7.2 190.4 %reduce-scatter.5.cloned.1.call-start = ((), (), s32[]{:S(2)}) async-start(), calls=%async_computation.3 | async-start | bytes 11796480 | tf_op jit(solution)/shard_map/reduce_scatter | solution.py:73
  9.7 12.3 %copy-start.3 = (bf16[2,4,128,512]{3,2,1,0:T(8,128)(2,1)}, bf16[2,4,128,512]{3,2,1,0:T(8,128)(2,1)S(1)}, u32[]{:S(2)}) copy-start(bf16[2,4,128,512]{3,2,1,0:T(8,128)(2,1)S(1)} %fusion.7) | copy-start | bytes 3145732
  9.7 6.1 %copy-start.9 = (bf16[2,4,128,512]{3,2,1,0:T(8,128)(2,1)S(1)}, bf16[2,4,128,512]{3,2,1,0:T(8,128)(2,1)}, u32[]{:S(2)}) copy-start(bf16[2,4,128,512]{3,2,1,0:T(8,128)(2,1)} %param.7) | copy-start | bytes 3145732
  9.8 4.5 collective-permute-start.1
  11.2 4.2 collective-permute-start
  28.5 333.6 %reduce-scatter.3.cloned.1.call-start = ((), (), s32[]{:S(2)}) async-start(), calls=%async_computation.2 | async-start | bytes 11796480 | tf_op jit(solution)/shard_map/reduce_scatter | solution.py:73
  28.7 2.3 copy-start.4
  28.7 5.9 %slice-start = ((s8[4718592]{0:T(1024)(128)(4,1)}), s8[4194304]{0:T(1024)(128)(4,1)S(1)}, s32[]{:S(2)}) async-start(s8[4718592]{0:T(1024)(128)(4,1)} %bitcast.305), calls=%async_computation.5 | async-start | bytes 8388608
  31.0 3.6 slice-start.1
  37.6 1.2 copy-start.10
  40.6 15.8 %copy-start.1 = (bf16[2,4,128,512]{3,2,1,0:T(8,128)(2,1)}, bf16[2,4,128,512]{3,2,1,0:T(8,128)(2,1)S(1)}, u32[]{:S(2)}) copy-start(bf16[2,4,128,512]{3,2,1,0:T(8,128)(2,1)S(1)} %fusion.14) | copy-start | bytes 3145732
  40.7 9.1 %collective-permute-start.3 = (bf16[2,1,128,512]{3,2,1,0:T(8,128)(2,1)S(1)}, bf16[2,1,128,512]{3,2,1,0:T(8,128)(2,1)S(1)}, u32[]{:S(2)}, u32[]{:S(2)}) collective-permute-start(bf16[2,1,128,512]{3,2,1,0:T(8,128)(2,1)S(1)} %get-tuple-element.5), channel_id=1, source_target_pairs={{4,0},{8,4},{12,8},{16,12},{20,16},{24,20},{28,24},{5,1},{9,5},{13... | collective-permute-start | bytes 786440 | tf_op jit(solution)/shard_map/ppermute | solution.py:15
  42.0 8.7 %collective-permute-start.2 = (bf16[2,1,128,512]{3,2,1,0:T(8,128)(2,1)S(1)}, bf16[2,1,128,512]{3,2,1,0:T(8,128)(2,1)S(1)}, u32[]{:S(2)}, u32[]{:S(2)}) collective-permute-start(bf16[2,1,128,512]{3,2,1,0:T(8,128)(2,1)S(1)} %get-tuple-element.6), channel_id=1, source_target_pairs={{0,4},{4,8},{8,12},{12,16},{16,20},{20,24},{24,28},{1,5},{5,9},{9,... | collective-permute-start | bytes 786440 | tf_op jit(solution)/shard_map/ppermute | solution.py:14
  62.8 390.5 %all-reduce.5.cloned.1.call-start = ((), (), s32[]{:S(2)}) async-start(), calls=%async_computation.4 | async-start | bytes 9437184 | tf_op jit(solution)/shard_map/psum | solution.py:74
  63.1 3.6 copy-start.2
  367.7 3.9 copy-start.8
  369.7 2.0 copy-start.5
  369.7 2.7 copy-start.7
  453.3 3.4 copy-start.6
Sparse Core Ops, SparseCore 0:
  28.6 168.9 reduce-scatter.4
  200.0 162.0 reduce-scatter.2
  365.5 87.8 all-reduce.4
where the time goes:
time: 465 us
  waiting for transfers between devices  369 us (79%)
  matrix products  48.3 us (10%)
  between operations  14.2 us (3%)
  starting transfers between devices  14.1 us (3%)
  other arithmetic  13 us (3%)
  local copies, waits for them, and re-layouts  6.17 us (1%)
    reduce_scatter x2, waiting for transfers between devices, settle(): lax.psum_scatter(grad_term, 'date', scatter_dimension=0, tiled=True)  289 us
    psum x1, waiting for transfers between devices, settle(): return lax.psum(share_rows, 'band')  77.7 us
    dot_general x18, matrix products, back_terms(): lax.dot_general(shifted_piece, weight[row_offset + 1, col_offset + 1], ((...  33.8 us
    dot_general x18, matrix products, weight_terms(): lax.dot_general(left_field, shifted_piece, (((0, 1, 2), (0, 1, 2)), ((),...  14.5 us
    ppermute x2, starting transfers between devices, extended(): before = lax.ppermute(last, axis, up)  10.8 us
    mul x2, other arithmetic, weight_terms(): return (stacked * grad_scale).reshape(-1, stacked.shape[2])  9.67 us
  transfers between devices with their start and end apart: 7, of which 5 were waited for; matrix products, arithmetic and copies ran while one was open for 10% of the time, Pallas kernels for 0%

commit v1 on v0

--- a/solution.py
+++ b/solution.py
@@ -71,7 +71,7 @@
 
 def settle(grad_term):
     share_rows = lax.psum_scatter(grad_term, "date", scatter_dimension=0, tiled=True)
-    return lax.psum(share_rows, "band")
+    return jnp.sum(lax.all_gather(share_rows, "band"), axis=0)
 
 
 def body(inputs, preact_one, preact_two, cotangent, weight_one, weight_two):

time: 465 us -> 581 us (1.25)
  waiting for transfers between devices: 369 us -> 481 us
  other arithmetic: 13 us -> 33.8 us
  matrix products: 48.3 us -> 37.6 us
    all_gather x0 -> x2, waiting for transfers between devices: none -> 180 us  [settle(): return jnp.sum(lax.all_gather(share_rows, 'band'), axis=0)]
    psum x1 -> x0, waiting for transfers between devices: 77.7 us -> none  [settle(): return lax.psum(share_rows, 'band')]
    reduce_sum x0 -> x2, other arithmetic: none -> 20.8 us  [settle(): return jnp.sum(lax.all_gather(share_rows, 'band'), axis=0)]
    dot_general x18, matrix products: 33.8 us -> 23.1 us  [back_terms(): lax.dot_general(shifted_piece, weight[row_offset + 1, col_offset + 1], ((...]
    reduce_scatter x2, waiting for transfers between devices: 289 us -> 299 us  [settle(): lax.psum_scatter(grad_term, 'date', scatter_dimension=0, tiled=True)]
  transfers between devices with their start and end apart: 7 -> 8, of which waited for: 5 -> 6; matrix products, arithmetic and copies ran while one was open for 10% -> 8% of each run, Pallas kernels for 0% -> 0%
where the time goes in v1:
time: 581 us
  waiting for transfers between devices  481 us (83%)
  matrix products  37.6 us (6%)
  other arithmetic  33.8 us (6%)
  between operations  14.2 us (2%)
  starting transfers between devices  14.1 us (2%)
    reduce_scatter x2, waiting for transfers between devices, settle(): lax.psum_scatter(grad_term, 'date', scatter_dimension=0, tiled=True)  299 us
    all_gather x2, waiting for transfers between devices, settle(): return jnp.sum(lax.all_gather(share_rows, 'band'), axis=0)  180 us
    dot_general x18, matrix products, back_terms(): lax.dot_general(shifted_piece, weight[row_offset + 1, col_offset + 1], ((...  23.1 us
    reduce_sum x2, other arithmetic, settle(): return jnp.sum(lax.all_gather(share_rows, 'band'), axis=0)  20.8 us
    dot_general x18, matrix products, weight_terms(): lax.dot_general(left_field, shifted_piece, (((0, 1, 2), (0, 1, 2)), ((),...  14.5 us
  transfers between devices with their start and end apart: 8, of which 6 were waited for; matrix products, arithmetic and copies ran while one was open for 8% of the time, Pallas kernels for 0%

profile of v1, /device:TPU:0, one launch (start us, length us, event | category | flops | bytes accessed | tf_op | source)
XLA Modules:
  0.0 581.0 jit_solution(4347240399177635503)
XLA Ops:
  7.2 2.5 fusion.7
  9.8 1.4 collective-permute-start.1
  11.2 3.0 collective-permute-start
  14.3 1.1 collective-permute-done
  15.8 1.0 fusion.31
  21.0 1.0 fusion.25
  23.6 4.8 broadcast_multiply_fusion
  28.7 2.2 fusion.109
  31.0 1.8 fusion.43
  32.8 1.8 fusion.39
  38.9 1.7 fusion.14
  40.6 1.3 collective-permute-start.3
  41.9 7.8 %collective-permute-start.2 = (bf16[2,1,128,512]{3,2,1,0:T(8,128)(2,1)S(1)}, bf16[2,1,128,512]{3,2,1,0:T(8,128)(2,1)S(1)}, u32[]{:S(2)}, u32[]{:S(2)}) collective-permute-start(bf16[2,1,128,512]{3,2,1,0:T(8,128)(2,1)S(1)} %get-tuple-element.4), channel_id=1, source_target_pairs={{0,4},{4,8},{8,12},{12,16},{16,20},{20,24},{24,28},{1,5},{5,9},{9,... | collective-permute-start | bytes 786440 | tf_op jit(solution)/shard_map/ppermute | solution.py:14
  58.0 4.9 broadcast_multiply_fusion.1
  62.9 134.7 %reduce-scatter.5.cloned.1.call-done = f32[1152,512]{1,0:T(8,128)} async-done(((f32[4608,512]{1,0:T(8,128)}), f32[1152,512]{1,0:T(8,128)}) %reduce-scatter.5.cloned.1.call-update) | async-done | bytes 2359312 | tf_op jit(solution)/shard_map/reduce_scatter | solution.py:73
  197.9 164.2 %reduce-scatter.3.cloned.1.call-done = f32[1152,512]{1,0:T(8,128)} async-done(((f32[4608,512]{1,0:T(8,128)}), f32[1152,512]{1,0:T(8,128)}) %reduce-scatter.3.cloned.1.call-update) | async-done | bytes 2359312 | tf_op jit(solution)/shard_map/reduce_scatter | solution.py:73
  362.1 2.2 fusion.99
  364.4 1.8 fusion.93
  366.2 1.8 fusion.94
  371.8 2.2 add_convert_fusion
  374.0 89.6 %all-gather.7.cloned.1.call-done = f32[9216,512]{1,0:T(8,128)} async-done(((f32[1152,512]{1,0:T(8,128)}), f32[9216,512]{1,0:T(8,128)}) %all-gather.7.cloned.1.call-update) | async-done | bytes 18874384 | tf_op jit(solution)/shard_map/all_gather | solution.py:74
  463.6 10.4 %reduce_sum.19 = f32[1152,512]{1,0:T(8,128)} reduce(f32[8,1152,512]{2,1,0:T(8,128)} %bitcast.307, f32[]{:T(128)} %constant.10.clone.1), dimensions={0}, to_apply=%region_3.4 | reduce | flops 4128768 | bytes 21233668 | tf_op jit(solution)/shard_map/reduce_sum | solution.py:74
  474.0 90.1 %all-gather.5.cloned.1.call-done = f32[9216,512]{1,0:T(8,128)} async-done(((f32[1152,512]{1,0:T(8,128)}), f32[9216,512]{1,0:T(8,128)}) %all-gather.5.cloned.1.call-update) | async-done | bytes 18874384 | tf_op jit(solution)/shard_map/all_gather | solution.py:74
  564.1 10.4 %reduce_sum.18 = f32[1152,512]{1,0:T(8,128)} reduce(f32[8,1152,512]{2,1,0:T(8,128)} %bitcast.308, f32[]{:T(128)} %constant.10.clone.1), dimensions={0}, to_apply=%region_1.2 | reduce | flops 4128768 | bytes 21233668 | tf_op jit(solution)/shard_map/reduce_sum | solution.py:74
  (65 shorter events, 23.0 us)
Async XLA Ops:
  7.2 43.9 %copy-start = (bf16[2,4,128,512]{3,2,1,0:T(8,128)(2,1)S(1)}, bf16[2,4,128,512]{3,2,1,0:T(8,128)(2,1)}, u32[]{:S(2)}) copy-start(bf16[2,4,128,512]{3,2,1,0:T(8,128)(2,1)} %param.6) | copy-start | bytes 3145732
  7.2 190.4 %reduce-scatter.5.cloned.1.call-start = ((), (), s32[]{:S(2)}) async-start(), calls=%async_computation.3 | async-start | bytes 11796480 | tf_op jit(solution)/shard_map/reduce_scatter | solution.py:73
  9.7 12.3 %copy-start.3 = (bf16[2,4,128,512]{3,2,1,0:T(8,128)(2,1)}, bf16[2,4,128,512]{3,2,1,0:T(8,128)(2,1)S(1)}, u32[]{:S(2)}) copy-start(bf16[2,4,128,512]{3,2,1,0:T(8,128)(2,1)S(1)} %fusion.7) | copy-start | bytes 3145732
  9.7 6.1 %copy-start.5 = (bf16[2,4,128,512]{3,2,1,0:T(8,128)(2,1)S(1)}, bf16[2,4,128,512]{3,2,1,0:T(8,128)(2,1)}, u32[]{:S(2)}) copy-start(bf16[2,4,128,512]{3,2,1,0:T(8,128)(2,1)} %param.7) | copy-start | bytes 3145732
  9.8 4.5 collective-permute-start.1
  11.2 4.2 collective-permute-start
  28.5 333.6 %reduce-scatter.3.cloned.1.call-start = ((), (), s32[]{:S(2)}) async-start(), calls=%async_computation.2 | async-start | bytes 11796480 | tf_op jit(solution)/shard_map/reduce_scatter | solution.py:73
  28.7 2.3 copy-start.4
  28.7 5.9 %slice-start = ((s8[4718592]{0:T(1024)(128)(4,1)}), s8[4194304]{0:T(1024)(128)(4,1)S(1)}, s32[]{:S(2)}) async-start(s8[4718592]{0:T(1024)(128)(4,1)} %bitcast.309), calls=%async_computation.6 | async-start | bytes 8388608
  31.0 3.6 slice-start.1
  37.6 1.2 copy-start.6
  40.6 15.8 %copy-start.1 = (bf16[2,4,128,512]{3,2,1,0:T(8,128)(2,1)}, bf16[2,4,128,512]{3,2,1,0:T(8,128)(2,1)S(1)}, u32[]{:S(2)}) copy-start(bf16[2,4,128,512]{3,2,1,0:T(8,128)(2,1)S(1)} %fusion.14) | copy-start | bytes 3145732
  40.6 9.1 %collective-permute-start.3 = (bf16[2,1,128,512]{3,2,1,0:T(8,128)(2,1)S(1)}, bf16[2,1,128,512]{3,2,1,0:T(8,128)(2,1)S(1)}, u32[]{:S(2)}, u32[]{:S(2)}) collective-permute-start(bf16[2,1,128,512]{3,2,1,0:T(8,128)(2,1)S(1)} %get-tuple-element.3), channel_id=1, source_target_pairs={{4,0},{8,4},{12,8},{16,12},{20,16},{24,20},{28,24},{5,1},{9,5},{13... | collective-permute-start | bytes 786440 | tf_op jit(solution)/shard_map/ppermute | solution.py:15
  41.9 8.7 %collective-permute-start.2 = (bf16[2,1,128,512]{3,2,1,0:T(8,128)(2,1)S(1)}, bf16[2,1,128,512]{3,2,1,0:T(8,128)(2,1)S(1)}, u32[]{:S(2)}, u32[]{:S(2)}) collective-permute-start(bf16[2,1,128,512]{3,2,1,0:T(8,128)(2,1)S(1)} %get-tuple-element.4), channel_id=1, source_target_pairs={{0,4},{4,8},{8,12},{12,16},{16,20},{20,24},{24,28},{1,5},{5,9},{9,... | collective-permute-start | bytes 786440 | tf_op jit(solution)/shard_map/ppermute | solution.py:14
  62.8 400.8 %all-gather.7.cloned.1.call-start = ((), (), s32[]{:S(2)}) async-start(), calls=%async_computation.5 | async-start | bytes 21233664 | tf_op jit(solution)/shard_map/all_gather | solution.py:74
  197.6 366.5 %all-gather.5.cloned.1.call-start = ((), (), s32[]{:S(2)}) async-start(), calls=%async_computation.4 | async-start | bytes 21233664 | tf_op jit(solution)/shard_map/all_gather | solution.py:74
  362.1 2.3 copy-start.2
  362.1 5.9 %slice-start.2 = ((s8[4718592]{0:T(1024)(128)(4,1)}), s8[4194304]{0:T(1024)(128)(4,1)S(1)}, s32[]{:S(2)}) async-start(s8[4718592]{0:T(1024)(128)(4,1)} %bitcast.311), calls=%async_computation.8 | async-start | bytes 8388608
  364.4 3.7 slice-start.3
Sparse Core Ops, SparseCore 0:
  28.6 168.9 reduce-scatter.4
  199.9 162.0 reduce-scatter.2
  364.0 99.5 all-gather.6
  465.3 98.7 all-gather.4
